TPU v7x, 256 devices: a whole 4x4x8 slice. The times are simulated.
256 devices in a mesh: seq: 64 (over z, x, core), head: 4 (over y).
Axes of the slice: x: 4, y: 4, z: 8, core: 2. Of those that a mesh axis runs over, the one named last changes fastest.
Arguments:
- features: bfloat16 [8192, 4096], P('seq', 'head'), may hold values from -6 to 6
- proj_weight: bfloat16 [4096, 4096], P(None, 'head'), may hold values from -0.09375 to 0.09375
- query_vectors: bfloat16 [8192, 4096], P('seq', 'head'), may hold values from -6 to 6
- key_vectors: bfloat16 [8192, 4096], P('seq', 'head'), may hold values from -6 to 6
Outputs:
- rotated_queries: bfloat16 [8192, 4096], P('seq', 'head')
- rotated_keys: bfloat16 [8192, 4096], P('seq', 'head')
All inputs are finite; a program needn't handle non-finite values.
Results may differ from a plain program's by a relative error of at most 0.0024.
Values may be sent and summed in bfloat16 or wider, within the bound.
No kernel may reach another device: no remote copies, remote signals or barrier semaphores. Data moves between devices by JAX's collectives and lax.ppermute only.
A program may use at most 128 MiB of HBM per device.

v0:
```python
import jax
import jax.numpy as jnp
from jax import lax
from jax.sharding import PartitionSpec as P

HEAD_DIM = 128


def entering(array, axis, combine, identity):
    count, place = (lax.axis_size(axis), lax.axis_index(axis))
    everything = lax.all_gather(array, axis)
    start = jnp.broadcast_to(jnp.asarray(identity, array.dtype), array.shape)

    def turn(k, before):
        reached = k < place
        new = combine(before, everything[k])
        return jnp.where(reached, new, before)

    return lax.fori_loop(0, count, turn, start)


def small_inverse(matrix):
    highest = lax.Precision.HIGHEST
    size = matrix.shape[-1]
    position = jnp.arange(size)
    strict = (position[:, None] < position[None, :]).astype(jnp.float32)
    eye_block = jnp.eye(size, dtype=jnp.float32)
    power = -2.0 * matrix * strict[None]
    result = eye_block[None] + power
    reach = 2
    while reach < size:
        power = jnp.einsum("hij,hjk->hik", power, power, precision=highest)
        result = result + jnp.einsum("hij,hjk->hik", result, power, precision=highest)
        reach = reach * 2
    return 2.0 * result


def triangle_inverse(matrix):
    highest = lax.Precision.HIGHEST
    size = matrix.shape[-1]
    if size <= 16:
        return small_inverse(matrix)
    half = size // 2
    first = triangle_inverse(matrix[:, :half, :half])
    second = triangle_inverse(matrix[:, half:, half:])
    coupling = matrix[:, :half, half:]
    middle = jnp.einsum("hij,hjk->hik", first, coupling, precision=highest)
    corner = -jnp.einsum("hij,hjk->hik", middle, second, precision=highest)
    lower_left = jnp.zeros((matrix.shape[0], size - half, half), jnp.float32)
    top = jnp.concatenate([first, corner], axis=2)
    bottom = jnp.concatenate([lower_left, second], axis=2)
    return jnp.concatenate([top, bottom], axis=1)


def upper_solve(matrix, right_side):
    highest = lax.Precision.HIGHEST
    rows = matrix.shape[1]
    size = min(128, rows)
    count = rows // size
    solved_blocks = []
    for i in reversed(range(count)):
        inverse_block = triangle_inverse(matrix)
        solved_blocks.append(
            jnp.einsum("hij,hjk->hik", inverse_block, right_side, precision=highest)
        )
    return jnp.concatenate(solved_blocks[::-1], axis=1)


def body(features, proj_weight, query_vectors, key_vectors):
    highest = lax.Precision.HIGHEST
    tok_rows = query_vectors.shape[0]
    width = proj_weight.shape[1]
    local_heads = width // HEAD_DIM
    raw_proj = jnp.dot(
        lax.all_gather(features, "head", axis=1, tiled=True),
        proj_weight,
        preferred_element_type=jnp.float32,
    )
    raw_proj = raw_proj.reshape(tok_rows, local_heads, HEAD_DIM)
    directions = raw_proj * lax.rsqrt(jnp.sum(raw_proj * raw_proj, axis=-1, keepdims=True) + 1e-06)
    reflectors = jnp.transpose(directions, (1, 0, 2))
    targets = jnp.concatenate(
        [
            query_vectors.reshape(tok_rows, local_heads, HEAD_DIM),
            key_vectors.reshape(tok_rows, local_heads, HEAD_DIM),
        ],
        axis=0,
    )
    targets = jnp.transpose(targets.astype(jnp.float32), (1, 0, 2))
    gram = jnp.einsum("hid,hjd->hij", reflectors, reflectors, precision=highest)
    position = jnp.arange(tok_rows)
    upper = (position[:, None] < position[None, :]).astype(jnp.float32)
    identity_tok = jnp.eye(tok_rows, dtype=jnp.float32)
    inverse_t = gram * upper[None] + 0.5 * identity_tok[None]
    projected = jnp.einsum("hid,htd->hit", reflectors, targets, precision=highest)
    target_pos = jnp.concatenate([position, position])
    keep = (position[:, None] <= target_pos[None, :]).astype(jnp.float32)
    masked = projected * keep[None]
    right_side = jnp.concatenate([masked, reflectors], axis=2)
    solved = upper_solve(inverse_t, right_side)
    weights_tok = solved[:, :, : 2 * tok_rows]
    factor = solved[:, :, 2 * tok_rows :]
    local_part = targets - jnp.einsum("hit,hid->htd", weights_tok, reflectors, precision=highest)
    identity = jnp.broadcast_to(
        jnp.eye(HEAD_DIM, dtype=jnp.float32), (local_heads, HEAD_DIM, HEAD_DIM)
    )
    block_product = identity - jnp.einsum("hid,hie->hde", reflectors, factor, precision=highest)

    def combine(earlier, later):
        return jnp.einsum("hde,hef->hdf", earlier, later, precision=highest)

    carried = entering(block_product, "seq", combine, identity)
    rotated = jnp.einsum("hde,hte->htd", carried, local_part, precision=highest)
    rotated = jnp.transpose(rotated, (1, 0, 2))
    rotated_queries = rotated[:tok_rows].reshape(tok_rows, width).astype(jnp.bfloat16)
    rotated_keys = rotated[tok_rows:].reshape(tok_rows, width).astype(jnp.bfloat16)
    return (rotated_queries, rotated_keys)


def solution(mesh):
    in_specs = (P("seq", "head"), P(None, "head"), P("seq", "head"), P("seq", "head"))
    out_specs = (P("seq", "head"), P("seq", "head"))
    return jax.shard_map(body, mesh=mesh, in_specs=in_specs, out_specs=out_specs, check_vma=False)
```

profile of v0, /device:TPU:1, one launch (start us, length us, event | category | flops | bytes accessed | tf_op | source)
XLA Modules:
  0.0 355.1 jit_solution(6094807427301237134)
XLA Ops:
  10.7 27.5 %all-gather.4.cloned.1.call-done = bf16[128,4096]{1,0:T(8,128)(2,1)} async-done(((bf16[128,1024]{1,0:T(8,128)(2,1)}), bf16[128,4096]{1,0:T(8,128)(2,1)}) %all-gather.4.cloned.1.call-update) | async-done | bytes 1048592 | tf_op jit(solution)/shard_map/all_gather | solution.py:75
  38.2 5.0 %fusion.124 = f32[128,1024]{1,0:T(8,128)S(1)} fusion(bf16[128,4096]{1,0:T(8,128)(2,1)} %all-gather.4.cloned.1.call-done, bf16[4096,1024]{1,0:T(8,128)(2,1)} %param.7), kind=kOutput, calls=%fused_computation.185 | convolution fusion | flops 1073741824 | bytes 9961472 | tf_op jit(solution)/shard_map/dot_general | solution.py:74
  64.4 2.9 convolution_subtract_fusion
  67.3 141.6 %all-gather.6.cloned.1.call-done = f32[512,128,128]{2,1,0:T(8,128)} async-done(((f32[8,128,128]{2,1,0:T(8,128)}), f32[512,128,128]{2,1,0:T(8,128)}) %all-gather.6.cloned.1.call-update) | async-done | bytes 33554448 | tf_op jit(solution)/shard_map/all_gather | solution.py:11
  208.9 136.5 %while.13 = (s32[]{:T(128)}, f32[8,128,128]{1,2,0:T(8,128)S(1)}, s32[]{:T(128)}, f32[64,8,128,128]{3,2,1,0:T(8,128)}, s32[]{:T(128)}) while((s32[]{:T(128)}, f32[8,128,128]{1,2,0:T(8,128)S(1)}, s32[]{:T(128)}, f32[64,8,128,128]{3,2,1,0:T(8,128)}, s32[]{:T(128)}) %tuple.48), condition=%wide.region_2.3_spmd, body=%wide.region_1.2_spmd.sunk | while | flops 201457664 | bytes 3145811 | solution.py:19
  208.9 2.1 fusion.247
  219.6 2.1 fusion.247
  230.3 2.1 fusion.247
  238.8 2.1 fusion.247
  240.9 2.1 fusion.247
  249.5 2.1 fusion.247
  260.1 2.1 fusion.247
  268.7 2.1 fusion.247
  279.3 2.1 fusion.247
  285.7 2.1 fusion.247
  287.8 2.1 fusion.247
  298.5 2.1 fusion.247
  304.9 2.1 fusion.247
  307.0 2.1 fusion.247
  317.7 2.1 fusion.247
  324.1 2.1 fusion.247
  326.2 2.1 fusion.247
  336.9 2.1 fusion.247
  343.3 2.1 fusion.247
  (210 shorter events, 122.1 us)
Async XLA Ops:
  7.2 31.0 %all-gather.4.cloned.1.call-start = ((), (), s32[]{:S(2)}) async-start(), calls=%async_computation | async-start | bytes 1310720 | tf_op jit(solution)/shard_map/all_gather | solution.py:75
  7.9 201.0 %all-gather.6.cloned.1.call-start = ((), (), s32[]{:S(2)}) async-start(), calls=%async_computation.1 | async-start | bytes 34078720 | tf_op jit(solution)/shard_map/all_gather | solution.py:11
  10.6 49.5 %copy-start = (bf16[128,8,128]{2,0,1:T(8,128)(2,1)}, bf16[128,8,128]{2,0,1:T(8,128)(2,1)S(1)}, u32[]{:S(2)}) copy-start(bf16[128,8,128]{2,0,1:T(8,128)(2,1)S(1)} %copy.41) | copy-start | bytes 786436
Sparse Core Ops, SparseCore 0:
  9.8 28.3 all-gather.3
  64.4 144.4 all-gather.5
where the time goes:
time: 358 us; the launch traced here: 355 us
  waiting for transfers between devices  170 us (47%)
  matrix products  160 us (45%)
  between operations  14.7 us (4%)
  local copies, waits for them, and re-layouts  7.25 us (2%)
    all_gather x1, waiting for transfers between devices, entering(): everything = lax.all_gather(array, axis)  142 us
    dot_general x64, matrix products, combine(): return jnp.einsum('hde,hef->hdf', earlier, later, precision=highest)  132 us
    all_gather x1, waiting for transfers between devices, body(): lax.all_gather(features, 'head', axis=1, tiled=True)  27.5 us
  transfers between devices with their start and end apart: 2, of which 2 were waited for; matrix products, arithmetic and copies ran while one was open for 2% of the time, Pallas kernels for 0%

commit v1 on v0

--- a/solution.py
+++ b/solution.py
@@ -1,3 +1,5 @@
+import functools
+
 import jax
 import jax.numpy as jnp
 from jax import lax
@@ -6,17 +8,30 @@
 HEAD_DIM = 128
 
 
-def entering(array, axis, combine, identity):
-    count, place = (lax.axis_size(axis), lax.axis_index(axis))
-    everything = lax.all_gather(array, axis)
+def entering(array, axis, count, combine, identity):
+    place = lax.axis_index(axis)
     start = jnp.broadcast_to(jnp.asarray(identity, array.dtype), array.shape)
-
-    def turn(k, before):
-        reached = k < place
-        new = combine(before, everything[k])
-        return jnp.where(reached, new, before)
-
-    return lax.fori_loop(0, count, turn, start)
+    span = array
+    before = None
+    shift = 1
+    while shift < count:
+        pairs = [(k, k + shift) for k in range(count - shift)]
+        arrived = lax.ppermute(span, axis, pairs)
+        reached = place >= shift
+        last = shift * 2 >= count
+        if before is None:
+            before = jnp.where(reached, arrived, start)
+            if not last:
+                span = jnp.where(reached, combine(arrived, span), span)
+        elif last:
+            before = jnp.where(reached, combine(arrived, before), before)
+        else:
+            width = array.shape[-1]
+            both = combine(arrived, jnp.concatenate([span, before], axis=-1))
+            span = jnp.where(reached, both[..., :width], span)
+            before = jnp.where(reached, both[..., width:], before)
+        shift = shift * 2
+    return before if before is not None else start
 
 
 def small_inverse(matrix):
@@ -66,7 +81,7 @@
     return jnp.concatenate(solved_blocks[::-1], axis=1)
 
 
-def body(features, proj_weight, query_vectors, key_vectors):
+def body(seq_count, features, proj_weight, query_vectors, key_vectors):
     highest = lax.Precision.HIGHEST
     tok_rows = query_vectors.shape[0]
     width = proj_weight.shape[1]
@@ -109,7 +124,7 @@
     def combine(earlier, later):
         return jnp.einsum("hde,hef->hdf", earlier, later, precision=highest)
 
-    carried = entering(block_product, "seq", combine, identity)
+    carried = entering(block_product, "seq", seq_count, combine, identity)
     rotated = jnp.einsum("hde,hte->htd", carried, local_part, precision=highest)
     rotated = jnp.transpose(rotated, (1, 0, 2))
     rotated_queries = rotated[:tok_rows].reshape(tok_rows, width).astype(jnp.bfloat16)
@@ -120,4 +135,4 @@
 def solution(mesh):
     in_specs = (P("seq", "head"), P(None, "head"), P("seq", "head"), P("seq", "head"))
     out_specs = (P("seq", "head"), P("seq", "head"))
-    return jax.shard_map(body, mesh=mesh, in_specs=in_specs, out_specs=out_specs, check_vma=False)
+    return jax.shard_map(functools.partial(body, mesh.shape["seq"]), mesh=mesh, in_specs=in_specs, out_specs=out_specs, check_vma=False)

time: 358 us -> 208 us (0.58)
  the two profiles are of different devices: /device:TPU:1 before, /device:TPU:35 now
where the time goes in v1:
time: 208 us
  waiting for transfers between devices  114 us (55%)
  matrix products  38.3 us (18%)
  starting transfers between devices  31.7 us (15%)
  between operations  14.8 us (7%)
  local copies, waits for them, and re-layouts  5.15 us (2%)
  other arithmetic  4.06 us (2%)
    ppermute x6, waiting for transfers between devices, entering(): arrived = lax.ppermute(span, axis, pairs)  86.6 us
    ppermute x6, starting transfers between devices, entering(): arrived = lax.ppermute(span, axis, pairs)  31.7 us
    all_gather x1, waiting for transfers between devices, body(): lax.all_gather(features, 'head', axis=1, tiled=True)  26.2 us
    dot_general x6, matrix products, combine(): return jnp.einsum('hde,hef->hdf', earlier, later, precision=highest)  10.7 us
    dot_general x24, matrix products, small_inverse(): power = jnp.einsum('hij,hjk->hik', power, power, precision=highest)  5.09 us
    dot_general x24, matrix products, small_inverse(): jnp.einsum('hij,hjk->hik', result, power, precision=highest)  5.05 us
    dot_general x1, matrix products, body(): jnp.dot(lax.all_gather(features, 'head', axis=1, tiled=True), proj_weight...  4.97 us
    unnamed x17, local copies, waits for them, and re-layouts  4.26 us
  transfers between devices with their start and end apart: 7, of which 7 were waited for; matrix products, arithmetic and copies ran while one was open for 3% of the time, Pallas kernels for 0%

profile of v1, /device:TPU:35, one launch (start us, length us, event | category | flops | bytes accessed | tf_op | source)
XLA Modules:
  0.0 207.6 jit_solution(11913831428166195170)
XLA Ops:
  9.2 1.1 copy.85
  10.8 26.2 %all-gather.2.cloned.1.call-done = bf16[128,4096]{1,0:T(8,128)(2,1)} async-done(((bf16[128,1024]{1,0:T(8,128)(2,1)}), bf16[128,4096]{1,0:T(8,128)(2,1)}) %all-gather.2.cloned.1.call-update) | async-done | bytes 1048592 | tf_op jit(solution)/shard_map/all_gather | solution.py:90
  37.0 5.0 %fusion.141 = f32[128,1024]{1,0:T(8,128)S(1)} fusion(bf16[128,4096]{1,0:T(8,128)(2,1)} %all-gather.2.cloned.1.call-done, bf16[4096,1024]{1,0:T(8,128)(2,1)} %param.5), kind=kOutput, calls=%fused_computation.212 | convolution fusion | flops 1073741824 | bytes 9961472 | tf_op jit(solution)/shard_map/dot_general | solution.py:89
  42.6 1.2 fusion.5
  59.5 1.7 fusion
  62.2 5.7 %collective-permute-start = (f32[8,128,128]{1,2,0:T(8,128)S(1)}, f32[8,128,128]{1,2,0:T(8,128)S(1)}, u32[]{:S(2)}, u32[]{:S(2)}) collective-permute-start(f32[8,128,128]{1,2,0:T(8,128)S(1)} %convolution_subtract_fusion.1), channel_id=1, source_target_pairs={{0,4},{4,8},{8,12},{12,16},{16,20},{20,24},{24,28},{28,32},{32,36}... | collective-permute-start | bytes 1572872 | tf_op jit(solution)/shard_map/ppermute | solution.py:19
  68.0 6.1 %collective-permute-done = f32[8,128,128]{1,2,0:T(8,128)S(1)} collective-permute-done((f32[8,128,128]{1,2,0:T(8,128)S(1)}, f32[8,128,128]{1,2,0:T(8,128)S(1)}, u32[]{:S(2)}, u32[]{:S(2)}) %collective-permute-start) | collective-permute-done | bytes 524320 | tf_op jit(solution)/shard_map/ppermute | solution.py:19
  74.1 1.8 convolution_select_fusion.1
  75.9 2.8 %collective-permute-start.1 = (f32[8,128,128]{1,2,0:T(8,128)S(1)}, f32[8,128,128]{1,2,0:T(8,128)}, u32[]{:S(2)}, u32[]{:S(2)}) collective-permute-start(f32[8,128,128]{1,2,0:T(8,128)S(1)} %convolution_select_fusion.1), channel_id=1, source_target_pairs={{0,8},{4,12},{8,16},{12,20},{16,24},{20,28},{24,32},{28,36},{32,40... | collective-permute-start | bytes 1572872 | tf_op jit(solution)/shard_map/ppermute | solution.py:19
  78.7 10.6 %collective-permute-done.1 = f32[8,128,128]{1,2,0:T(8,128)} collective-permute-done((f32[8,128,128]{1,2,0:T(8,128)S(1)}, f32[8,128,128]{1,2,0:T(8,128)}, u32[]{:S(2)}, u32[]{:S(2)}) %collective-permute-start.1) | collective-permute-done | bytes 524320 | tf_op jit(solution)/shard_map/ppermute | solution.py:19
  89.3 2.0 fusion.15
  91.3 1.1 slice_select_fusion.7
  92.5 4.6 %collective-permute-start.2 = (f32[8,128,128]{1,2,0:T(8,128)}, f32[8,128,128]{1,2,0:T(8,128)S(1)}, u32[]{:S(2)}, u32[]{:S(2)}) collective-permute-start(f32[8,128,128]{1,2,0:T(8,128)} %get-tuple-element.15), channel_id=1, source_target_pairs={{0,16},{4,20},{8,24},{12,28},{16,32},{20,36},{24,40},{28,44},{32,4... | collective-permute-start | bytes 1572872 | tf_op jit(solution)/shard_map/ppermute | solution.py:19
  97.1 10.6 %collective-permute-done.2 = f32[8,128,128]{1,2,0:T(8,128)S(1)} collective-permute-done((f32[8,128,128]{1,2,0:T(8,128)}, f32[8,128,128]{1,2,0:T(8,128)S(1)}, u32[]{:S(2)}, u32[]{:S(2)}) %collective-permute-start.2) | collective-permute-done | bytes 524320 | tf_op jit(solution)/shard_map/ppermute | solution.py:19
  107.7 2.2 %fusion.19 = f32[8,128,256]{1,2,0:T(8,128)S(1)} fusion(f32[8,128,128]{1,2,0:T(8,128)S(1)} %collective-permute-done.2, f32[8,128,128]{1,2,0:T(8,128)} %get-tuple-element.14, f32[8,128,128]{1,2,0:T(8,128)} %get-tuple-element.15), kind=kOutput, calls=%fused_computation.57 | convolution fusion | flops 402915328 | bytes 2621440 | tf_op jit(solution)/shard_map/hde,hef->hdf/dot_general | solution.py:125
  110.8 3.2 %collective-permute-start.3 = (f32[8,128,128]{1,2,0:T(8,128)}, f32[8,128,128]{1,2,0:T(8,128)S(1)}, u32[]{:S(2)}, u32[]{:S(2)}) collective-permute-start(f32[8,128,128]{1,2,0:T(8,128)} %get-tuple-element.13), channel_id=1, source_target_pairs={{0,32},{4,36},{8,40},{12,44},{16,48},{20,52},{24,56},{28,60},{32,6... | collective-permute-start | bytes 1572872 | tf_op jit(solution)/shard_map/ppermute | solution.py:19
  114.0 8.6 %collective-permute-done.3 = f32[8,128,128]{1,2,0:T(8,128)S(1)} collective-permute-done((f32[8,128,128]{1,2,0:T(8,128)}, f32[8,128,128]{1,2,0:T(8,128)S(1)}, u32[]{:S(2)}, u32[]{:S(2)}) %collective-permute-start.3) | collective-permute-done | bytes 524320 | tf_op jit(solution)/shard_map/ppermute | solution.py:19
  122.6 2.0 fusion.23
  124.8 9.3 %collective-permute-start.4 = (f32[8,128,128]{1,2,0:T(8,128)S(1)}, f32[8,128,128]{1,2,0:T(8,128)}, u32[]{:S(2)}, u32[]{:S(2)}) collective-permute-start(f32[8,128,128]{1,2,0:T(8,128)S(1)} %get-tuple-element.11), channel_id=1, source_target_pairs={{0,64},{4,68},{8,72},{12,76},{16,80},{20,84},{24,88},{28,92},{32,9... | collective-permute-start | bytes 1572872 | tf_op jit(solution)/shard_map/ppermute | solution.py:19
  134.1 32.4 %collective-permute-done.4 = f32[8,128,128]{1,2,0:T(8,128)} collective-permute-done((f32[8,128,128]{1,2,0:T(8,128)S(1)}, f32[8,128,128]{1,2,0:T(8,128)}, u32[]{:S(2)}, u32[]{:S(2)}) %collective-permute-start.4) | collective-permute-done | bytes 524320 | tf_op jit(solution)/shard_map/ppermute | solution.py:19
  166.6 2.0 fusion.27
  169.8 6.0 %collective-permute-start.5 = (f32[8,128,128]{1,2,0:T(8,128)}, f32[8,128,128]{1,2,0:T(8,128)S(1)}, u32[]{:S(2)}, u32[]{:S(2)}) collective-permute-start(f32[8,128,128]{1,2,0:T(8,128)} %slice_select_fusion.2), channel_id=1, source_target_pairs={{0,128},{4,132},{8,136},{12,140},{16,144},{20,148},{24,152},{28,15... | collective-permute-start | bytes 1572872 | tf_op jit(solution)/shard_map/ppermute | solution.py:19
  175.8 3.0 %convolution_subtract_fusion = f32[8,256,128]{2,1,0:T(8,128)S(1)} fusion(f32[8,128,128]{2,1,0:T(8,128)S(1)} %fusion.31, f32[8,128,384]{2,1,0:T(8,128)S(1)} %fusion, bf16[128,8,128]{2,0,1:T(8,128)(2,1)S(1)} %copy.88, bf16[128,8,128]{2,0,1:T(8,128)(2,1)} %copy-done.4), kind=kOutput, calls=%fused_computation.4 | convolution fusion | flops 404226048 | bytes 3145728 | tf_op jit(solution)/shard_map/hit,hid->htd/dot_general | solution.py:118
  178.8 18.4 %collective-permute-done.5 = f32[8,128,128]{1,2,0:T(8,128)S(1)} collective-permute-done((f32[8,128,128]{1,2,0:T(8,128)}, f32[8,128,128]{1,2,0:T(8,128)S(1)}, u32[]{:S(2)}, u32[]{:S(2)}) %collective-permute-start.5) | collective-permute-done | bytes 524320 | tf_op jit(solution)/shard_map/ppermute | solution.py:19
  (110 shorter events, 25.0 us)
Async XLA Ops:
  7.2 29.8 %all-gather.2.cloned.1.call-start = ((), (), s32[]{:S(2)}) async-start(), calls=%async_computation | async-start | bytes 1310720 | tf_op jit(solution)/shard_map/all_gather | solution.py:90
  10.5 48.3 %copy-start.4 = (bf16[128,8,128]{2,0,1:T(8,128)(2,1)}, bf16[128,8,128]{2,0,1:T(8,128)(2,1)S(1)}, u32[]{:S(2)}) copy-start(bf16[128,8,128]{2,0,1:T(8,128)(2,1)S(1)} %copy.87) | copy-start | bytes 786436
  62.2 5.8 %copy-start.5 = (f32[8,128,128]{1,2,0:T(8,128)}, f32[8,128,128]{1,2,0:T(8,128)S(1)}, u32[]{:S(2)}) copy-start(f32[8,128,128]{1,2,0:T(8,128)S(1)} %convolution_subtract_fusion.1) | copy-start | bytes 1572868
  62.2 11.9 %collective-permute-start = (f32[8,128,128]{1,2,0:T(8,128)S(1)}, f32[8,128,128]{1,2,0:T(8,128)S(1)}, u32[]{:S(2)}, u32[]{:S(2)}) collective-permute-start(f32[8,128,128]{1,2,0:T(8,128)S(1)} %convolution_subtract_fusion.1), channel_id=1, source_target_pairs={{0,4},{4,8},{8,12},{12,16},{16,20},{20,24},{24,28},{28,32},{32,36}... | collective-permute-start | bytes 1572872 | tf_op jit(solution)/shard_map/ppermute | solution.py:19
  75.9 13.4 %collective-permute-start.1 = (f32[8,128,128]{1,2,0:T(8,128)S(1)}, f32[8,128,128]{1,2,0:T(8,128)}, u32[]{:S(2)}, u32[]{:S(2)}) collective-permute-start(f32[8,128,128]{1,2,0:T(8,128)S(1)} %convolution_select_fusion.1), channel_id=1, source_target_pairs={{0,8},{4,12},{8,16},{12,20},{16,24},{20,28},{24,32},{28,36},{32,40... | collective-permute-start | bytes 1572872 | tf_op jit(solution)/shard_map/ppermute | solution.py:19
  92.5 17.4 %copy-start = (f32[8,128,128]{1,2,0:T(8,128)S(1)}, f32[8,128,128]{1,2,0:T(8,128)}, u32[]{:S(2)}) copy-start(f32[8,128,128]{1,2,0:T(8,128)} %get-tuple-element.14) | copy-start | bytes 1572868
  92.5 15.2 %collective-permute-start.2 = (f32[8,128,128]{1,2,0:T(8,128)}, f32[8,128,128]{1,2,0:T(8,128)S(1)}, u32[]{:S(2)}, u32[]{:S(2)}) collective-permute-start(f32[8,128,128]{1,2,0:T(8,128)} %get-tuple-element.15), channel_id=1, source_target_pairs={{0,16},{4,20},{8,24},{12,28},{16,32},{20,36},{24,40},{28,44},{32,4... | collective-permute-start | bytes 1572872 | tf_op jit(solution)/shard_map/ppermute | solution.py:19
  110.8 11.8 %copy-start.1 = (f32[8,128,128]{1,2,0:T(8,128)}, f32[8,128,128]{1,2,0:T(8,128)S(1)}, u32[]{:S(2)}) copy-start(f32[8,128,128]{1,2,0:T(8,128)S(1)} %get-tuple-element.12) | copy-start | bytes 1572868
  110.8 11.8 %collective-permute-start.3 = (f32[8,128,128]{1,2,0:T(8,128)}, f32[8,128,128]{1,2,0:T(8,128)S(1)}, u32[]{:S(2)}, u32[]{:S(2)}) collective-permute-start(f32[8,128,128]{1,2,0:T(8,128)} %get-tuple-element.13), channel_id=1, source_target_pairs={{0,32},{4,36},{8,40},{12,44},{16,48},{20,52},{24,56},{28,60},{32,6... | collective-permute-start | bytes 1572872 | tf_op jit(solution)/shard_map/ppermute | solution.py:19
  124.8 41.8 %collective-permute-start.4 = (f32[8,128,128]{1,2,0:T(8,128)S(1)}, f32[8,128,128]{1,2,0:T(8,128)}, u32[]{:S(2)}, u32[]{:S(2)}) collective-permute-start(f32[8,128,128]{1,2,0:T(8,128)S(1)} %get-tuple-element.11), channel_id=1, source_target_pairs={{0,64},{4,68},{8,72},{12,76},{16,80},{20,84},{24,88},{28,92},{32,9... | collective-permute-start | bytes 1572872 | tf_op jit(solution)/shard_map/ppermute | solution.py:19
  168.6 1.2 copy-start.2
  169.8 27.4 %collective-permute-start.5 = (f32[8,128,128]{1,2,0:T(8,128)}, f32[8,128,128]{1,2,0:T(8,128)S(1)}, u32[]{:S(2)}, u32[]{:S(2)}) collective-permute-start(f32[8,128,128]{1,2,0:T(8,128)} %slice_select_fusion.2), channel_id=1, source_target_pairs={{0,128},{4,132},{8,136},{12,140},{16,144},{20,148},{24,152},{28,15... | collective-permute-start | bytes 1572872 | tf_op jit(solution)/shard_map/ppermute | solution.py:19
  175.8 21.4 %copy-start.3 = (f32[8,128,256]{1,2,0:T(8,128)S(1)}, f32[8,128,256]{1,2,0:T(8,128)}, u32[]{:S(2)}) copy-start(f32[8,128,256]{1,2,0:T(8,128)} %copy-done.2) | copy-start | bytes 3145732
Sparse Core Ops, SparseCore 0:
  9.8 27.1 all-gather.1

commit v2 on v1

--- a/solution.py
+++ b/solution.py
@@ -32,6 +32,59 @@
             before = jnp.where(reached, both[..., width:], before)
         shift = shift * 2
     return before if before is not None else start
+
+
+def paired_entering(array, axis, count, combine, identity):
+    place = lax.axis_index(axis)
+    core = place % 2
+    first = core == 0
+    half = array.shape[0] // 2
+    swap = [(k, k ^ 1) for k in range(count)]
+    mate = lax.ppermute(array, axis, swap)
+    chip = combine(jnp.where(first, array, mate), jnp.where(first, mate, array))
+    inner = jnp.where(first, jnp.broadcast_to(identity, array.shape), mate)
+    mine = lax.dynamic_slice_in_dim(chip, core * half, half, 0)
+    start = jnp.broadcast_to(identity, mine.shape)
+    span = mine
+    before = start
+    shift = 2
+    while shift < count:
+        pairs = [(k, k + shift) for k in range(count - shift)]
+        arrived = lax.ppermute(span, axis, pairs)
+        reached = place >= shift
+        last = shift * 2 >= count
+        if shift == 2:
+            before = jnp.where(reached, arrived, start)
+            if not last:
+                span = jnp.where(reached, combine(arrived, span), span)
+        elif last:
+            before = jnp.where(reached, combine(arrived, before), before)
+        else:
+            width = array.shape[-1]
+            both = combine(arrived, jnp.concatenate([span, before], axis=-1))
+            span = jnp.where(reached, both[..., :width], span)
+            before = jnp.where(reached, both[..., width:], before)
+        shift = shift * 2
+    other = lax.ppermute(before, axis, swap)
+    full = jnp.where(
+        first,
+        jnp.concatenate([before, other], axis=0),
+        jnp.concatenate([other, before], axis=0),
+    )
+    return combine(full, inner)
+
+
+def gathered_projection(features, proj_weight, axis, count):
+    place = lax.axis_index(axis)
+    width = features.shape[1]
+    rows = lambda owner: lax.dynamic_slice_in_dim(proj_weight, owner * width, width, 0)
+    total = jnp.dot(features, rows(place), preferred_element_type=jnp.float32)
+    for step in range(1, count):
+        pairs = [(k, (k + step) % count) for k in range(count)]
+        part = lax.ppermute(features, axis, pairs)
+        owner = (place + count - step) % count
+        total = total + jnp.dot(part, rows(owner), preferred_element_type=jnp.float32)
+    return total
 
 
 def small_inverse(matrix):
@@ -81,16 +134,12 @@
     return jnp.concatenate(solved_blocks[::-1], axis=1)
 
 
-def body(seq_count, features, proj_weight, query_vectors, key_vectors):
+def body(seq_count, head_count, features, proj_weight, query_vectors, key_vectors):
     highest = lax.Precision.HIGHEST
     tok_rows = query_vectors.shape[0]
     width = proj_weight.shape[1]
     local_heads = width // HEAD_DIM
-    raw_proj = jnp.dot(
-        lax.all_gather(features, "head", axis=1, tiled=True),
-        proj_weight,
-        preferred_element_type=jnp.float32,
-    )
+    raw_proj = gathered_projection(features, proj_weight, "head", head_count)
     raw_proj = raw_proj.reshape(tok_rows, local_heads, HEAD_DIM)
     directions = raw_proj * lax.rsqrt(jnp.sum(raw_proj * raw_proj, axis=-1, keepdims=True) + 1e-06)
     reflectors = jnp.transpose(directions, (1, 0, 2))
@@ -124,7 +173,10 @@
     def combine(earlier, later):
         return jnp.einsum("hde,hef->hdf", earlier, later, precision=highest)
 
-    carried = entering(block_product, "seq", seq_count, combine, identity)
+    if seq_count % 2 == 0 and local_heads % 2 == 0:
+        carried = paired_entering(block_product, "seq", seq_count, combine, identity[0])
+    else:
+        carried = entering(block_product, "seq", seq_count, combine, identity)
     rotated = jnp.einsum("hde,hte->htd", carried, local_part, precision=highest)
     rotated = jnp.transpose(rotated, (1, 0, 2))
     rotated_queries = rotated[:tok_rows].reshape(tok_rows, width).astype(jnp.bfloat16)
@@ -135,4 +187,4 @@
 def solution(mesh):
     in_specs = (P("seq", "head"), P(None, "head"), P("seq", "head"), P("seq", "head"))
     out_specs = (P("seq", "head"), P("seq", "head"))
-    return jax.shard_map(functools.partial(body, mesh.shape["seq"]), mesh=mesh, in_specs=in_specs, out_specs=out_specs, check_vma=False)
+    return jax.shard_map(functools.partial(body, mesh.shape["seq"], mesh.shape["head"]), mesh=mesh, in_specs=in_specs, out_specs=out_specs, check_vma=False)

time: 208 us -> 133 us (0.64)
  the two profiles are of different devices: /device:TPU:35 before, /device:TPU:1 now
where the time goes in v2:
time: 133 us; the launch traced here: 131 us
  starting transfers between devices  52.7 us (40%)
  matrix products  40.2 us (30%)
  waiting for transfers between devices  27.6 us (21%)
  other arithmetic  5.33 us (4%)
  local copies, waits for them, and re-layouts  3.29 us (2%)
  between operations  1.5 us (1%)
    ppermute x5, starting transfers between devices, paired_entering(): arrived = lax.ppermute(span, axis, pairs)  44.2 us
    ppermute x5, waiting for transfers between devices, paired_entering(): arrived = lax.ppermute(span, axis, pairs)  18.9 us
    dot_general x7, matrix products, combine(): return jnp.einsum('hde,hef->hdf', earlier, later, precision=highest)  9.27 us
    ppermute x3, waiting for transfers between devices, gathered_projection(): part = lax.ppermute(features, axis, pairs)  7.22 us
    dot_general x3, matrix products, gathered_projection(): jnp.dot(part, rows(owner), preferred_element_type=jnp.float32)  7.03 us
    dot_general x24, matrix products, small_inverse(): power = jnp.einsum('hij,hjk->hik', power, power, precision=highest)  5.09 us
    dot_general x24, matrix products, small_inverse(): jnp.einsum('hij,hjk->hik', result, power, precision=highest)  5.05 us
    ppermute x3, starting transfers between devices, gathered_projection(): part = lax.ppermute(features, axis, pairs)  4.67 us
  transfers between devices with their start and end apart: 10, of which 8 were waited for; matrix products, arithmetic and copies ran while one was open for 7% of the time, Pallas kernels for 0%

profile of v2, /device:TPU:1, one launch (start us, length us, event | category | flops | bytes accessed | tf_op | source)
XLA Modules:
  0.0 130.6 jit_solution(17059930573905971716)
XLA Ops:
  0.6 3.6 %collective-permute-start.2 = (bf16[128,1024]{1,0:T(8,128)(2,1)}, bf16[128,1024]{1,0:T(8,128)(2,1)S(1)}, u32[]{:S(2)}, u32[]{:S(2)}) collective-permute-start(bf16[128,1024]{1,0:T(8,128)(2,1)} %param.4), channel_id=1, source_target_pairs={{0,3},{1,0},{2,1},{3,2},{4,7},{5,4},{6,5},{7,6},{8,11},{9,8},{10,9... | collective-permute-start | bytes 786440 | tf_op jit(solution)/shard_map/ppermute | solution.py:84
  5.4 2.4 %fusion.6 = f32[1024,128]{1,0:T(8,128)S(1)} fusion(bf16[128,1024]{1,0:T(8,128)(2,1)} %param.4, bf16[4096,1024]{1,0:T(8,128)(2,1)} %param.5, s32[]{:T(128)S(6)} %select_n.102), kind=kOutput, calls=%fused_computation.6 | convolution fusion | flops 268435456 | bytes 2883588 | tf_op jit(solution)/shard_map/dot_general | solution.py:81
  8.0 7.0 %collective-permute-done.2 = bf16[128,1024]{1,0:T(8,128)(2,1)S(1)} collective-permute-done((bf16[128,1024]{1,0:T(8,128)(2,1)}, bf16[128,1024]{1,0:T(8,128)(2,1)S(1)}, u32[]{:S(2)}, u32[]{:S(2)}) %collective-permute-start.2) | collective-permute-done | bytes 262176 | tf_op jit(solution)/shard_map/ppermute | solution.py:84
  15.1 2.3 %fusion = f32[1024,128]{1,0:T(8,128)S(1)} fusion(bf16[128,1024]{1,0:T(8,128)(2,1)S(1)} %collective-permute-done.2, bf16[4096,1024]{1,0:T(8,128)(2,1)} %param.5, s32[]{:T(128)S(6)} %select_n.108), kind=kOutput, calls=%fused_computation | convolution fusion | flops 268435456 | bytes 2883588 | tf_op jit(solution)/shard_map/dot_general | solution.py:86
  17.4 2.3 %fusion.2 = f32[1024,128]{1,0:T(8,128)S(1)} fusion(bf16[128,1024]{1,0:T(8,128)(2,1)S(1)} %collective-permute-done.1, bf16[4096,1024]{1,0:T(8,128)(2,1)} %param.5, s32[]{:T(128)S(6)} %select_n.106), kind=kOutput, calls=%fused_computation.2 | convolution fusion | flops 268435456 | bytes 2883588 | tf_op jit(solution)/shard_map/dot_general | solution.py:86
  19.9 2.4 %multiply_reduce_fusion = (f32[128,8]{0,1:T(8,128)S(1)}, f32[1024,128]{1,0:T(8,128)S(1)}) fusion(f32[1024,128]{1,0:T(8,128)S(1)} %fusion, f32[1024,128]{1,0:T(8,128)S(1)} %fusion.2, f32[1024,128]{1,0:T(8,128)S(1)} %fusion.6, bf16[128,1024]{1,0:T(8,128)(2,1)} %collective-permute-done, bf16[4096,1024]{1,0:T(8,128)(2,1)} %param.5, s32[]{:T(128)S(6)} %select_n.104), kind=kOutput, calls=%fused_computation.104 | convolution fusion | flops 269089792 | bytes 4460548 | tf_op jit(solution)/shard_map/dot_general | solution.py:86
  42.4 1.6 %collective-permute-start.3 = (f32[8,128,128]{2,1,0:T(8,128)S(1)}, f32[8,128,128]{2,1,0:T(8,128)S(1)}, u32[]{:S(2)}, u32[]{:S(2)}) collective-permute-start(f32[8,128,128]{2,1,0:T(8,128)S(1)} %convolution_subtract_fusion.1), channel_id=1, source_target_pairs={{0,4},{4,0},{8,12},{12,8},{16,20},{20,16},{24,28},{28,24},{32,36},... | collective-permute-start | bytes 1572872 | tf_op jit(solution)/shard_map/ppermute | solution.py:43
  43.9 1.5 %collective-permute-done.3 = f32[8,128,128]{2,1,0:T(8,128)S(1)} collective-permute-done((f32[8,128,128]{2,1,0:T(8,128)S(1)}, f32[8,128,128]{2,1,0:T(8,128)S(1)}, u32[]{:S(2)}, u32[]{:S(2)}) %collective-permute-start.3) | collective-permute-done | bytes 524320 | tf_op jit(solution)/shard_map/ppermute | solution.py:43
  46.2 3.1 %collective-permute-start.4 = (f32[4,128,128]{2,1,0:T(8,128)S(1)}, f32[4,128,128]{2,1,0:T(8,128)S(1)}, u32[]{:S(2)}, u32[]{:S(2)}) collective-permute-start(f32[4,128,128]{2,1,0:T(8,128)S(1)} %constant_dynamic-slice_fusion), channel_id=1, source_target_pairs={{0,8},{4,12},{8,16},{12,20},{16,24},{20,28},{24,32},{28,36},{32,40... | collective-permute-start | bytes 786440 | tf_op jit(solution)/shard_map/ppermute | solution.py:53
  49.3 5.2 %collective-permute-done.4 = f32[4,128,128]{2,1,0:T(8,128)S(1)} collective-permute-done((f32[4,128,128]{2,1,0:T(8,128)S(1)}, f32[4,128,128]{2,1,0:T(8,128)S(1)}, u32[]{:S(2)}, u32[]{:S(2)}) %collective-permute-start.4) | collective-permute-done | bytes 262176 | tf_op jit(solution)/shard_map/ppermute | solution.py:53
  56.1 6.3 %collective-permute-start.5 = (f32[4,128,128]{2,1,0:T(8,128)S(1)}, f32[4,128,128]{2,1,0:T(8,128)}, u32[]{:S(2)}, u32[]{:S(2)}) collective-permute-start(f32[4,128,128]{2,1,0:T(8,128)S(1)} %convolution_select_fusion.1), channel_id=1, source_target_pairs={{0,16},{4,20},{8,24},{12,28},{16,32},{20,36},{24,40},{28,44},{32,4... | collective-permute-start | bytes 786440 | tf_op jit(solution)/shard_map/ppermute | solution.py:53
  62.5 3.7 %collective-permute-done.5 = f32[4,128,128]{2,1,0:T(8,128)} collective-permute-done((f32[4,128,128]{2,1,0:T(8,128)S(1)}, f32[4,128,128]{2,1,0:T(8,128)}, u32[]{:S(2)}, u32[]{:S(2)}) %collective-permute-start.5) | collective-permute-done | bytes 262176 | tf_op jit(solution)/shard_map/ppermute | solution.py:53
  68.8 8.3 %collective-permute-start.6 = (f32[4,128,128]{2,1,0:T(8,128)S(1)}, f32[4,128,128]{2,1,0:T(8,128)}, u32[]{:S(2)}, u32[]{:S(2)}) collective-permute-start(f32[4,128,128]{2,1,0:T(8,128)S(1)} %get-tuple-element.9), channel_id=1, source_target_pairs={{0,32},{4,36},{8,40},{12,44},{16,48},{20,52},{24,56},{28,60},{32,6... | collective-permute-start | bytes 786440 | tf_op jit(solution)/shard_map/ppermute | solution.py:53
  77.1 2.9 %collective-permute-done.6 = f32[4,128,128]{2,1,0:T(8,128)} collective-permute-done((f32[4,128,128]{2,1,0:T(8,128)S(1)}, f32[4,128,128]{2,1,0:T(8,128)}, u32[]{:S(2)}, u32[]{:S(2)}) %collective-permute-start.6) | collective-permute-done | bytes 262176 | tf_op jit(solution)/shard_map/ppermute | solution.py:53
  81.5 2.0 %slice_select_fusion.3 = (f32[4,128,128]{2,1,0:T(8,128)}, f32[4,128,128]{2,1,0:T(8,128)}) fusion(f32[4,128,128]{2,1,0:T(8,128)} %copy-done.5, f32[4,128,256]{2,1,0:T(8,128)S(1)} %fusion.49, pred[]{:T(512)S(6)} %ge.17, f32[4,128,128]{2,1,0:T(8,128)} %copy-done.6), kind=kLoop, calls=%fused_computation.109 | loop fusion | flops 131072 | bytes 1572865 | tf_op jit(solution)/shard_map/jit(_where)/select_n | solution.py:66
  83.5 5.2 %collective-permute-start.7 = (f32[4,128,128]{2,1,0:T(8,128)}, f32[4,128,128]{2,1,0:T(8,128)}, u32[]{:S(2)}, u32[]{:S(2)}) collective-permute-start(f32[4,128,128]{2,1,0:T(8,128)} %get-tuple-element.7), channel_id=1, source_target_pairs={{0,64},{4,68},{8,72},{12,76},{16,80},{20,84},{24,88},{28,92},{32,9... | collective-permute-start | bytes 786440 | tf_op jit(solution)/shard_map/ppermute | solution.py:53
  88.7 2.9 %collective-permute-done.7 = f32[4,128,128]{2,1,0:T(8,128)} collective-permute-done((f32[4,128,128]{2,1,0:T(8,128)}, f32[4,128,128]{2,1,0:T(8,128)}, u32[]{:S(2)}, u32[]{:S(2)}) %collective-permute-start.7) | collective-permute-done | bytes 262176 | tf_op jit(solution)/shard_map/ppermute | solution.py:53
  91.6 1.7 %fusion.53 = f32[4,128,256]{2,1,0:T(8,128)S(1)} fusion(f32[4,128,128]{2,1,0:T(8,128)} %collective-permute-done.7, f32[4,128,128]{2,1,0:T(8,128)} %get-tuple-element.6, f32[4,128,128]{2,1,0:T(8,128)} %get-tuple-element.7), kind=kOutput, calls=%fused_computation.88 | convolution fusion | flops 201457664 | bytes 1310720 | tf_op jit(solution)/shard_map/hde,hef->hdf/dot_general | solution.py:174
  94.1 1.7 %slice_select_fusion.2 = f32[4,128,128]{2,1,0:T(8,128)} fusion(f32[4,128,128]{2,1,0:T(8,128)} %get-tuple-element.7, f32[4,128,256]{2,1,0:T(8,128)S(1)} %fusion.53, pred[]{:T(512)S(6)} %ge.16), kind=kLoop, calls=%fused_computation.108 | loop fusion | flops 65536 | bytes 786433 | tf_op jit(solution)/shard_map/jit(_where)/select_n | solution.py:65
  95.8 21.2 %collective-permute-start.8 = (f32[4,128,128]{2,1,0:T(8,128)}, f32[4,128,128]{2,1,0:T(8,128)}, u32[]{:S(2)}, u32[]{:S(2)}) collective-permute-start(f32[4,128,128]{2,1,0:T(8,128)} %slice_select_fusion.2), channel_id=1, source_target_pairs={{0,128},{4,132},{8,136},{12,140},{16,144},{20,148},{24,152},{28,15... | collective-permute-start | bytes 786440 | tf_op jit(solution)/shard_map/ppermute | solution.py:53
  117.0 4.2 %collective-permute-done.8 = f32[4,128,128]{2,1,0:T(8,128)} collective-permute-done((f32[4,128,128]{2,1,0:T(8,128)}, f32[4,128,128]{2,1,0:T(8,128)}, u32[]{:S(2)}, u32[]{:S(2)}) %collective-permute-start.8) | collective-permute-done | bytes 262176 | tf_op jit(solution)/shard_map/ppermute | solution.py:53
  121.2 1.7 %convolution_select_fusion = f32[4,128,128]{2,1,0:T(8,128)S(1)} fusion(f32[4,128,128]{2,1,0:T(8,128)} %collective-permute-done.8, f32[4,128,128]{2,1,0:T(8,128)} %get-tuple-element.6, f32[4,128,256]{2,1,0:T(8,128)} %copy-done.9, pred[]{:T(512)S(6)} %ge.16, pred[]{:T(512)S(6)} %ge.15), kind=kOutput, calls=%fused_computation.22 | convolution fusion | flops 100859904 | bytes 1574400 | tf_op jit(solution)/shard_map/hde,hef->hdf/dot_general | solution.py:174
  122.9 2.2 %collective-permute-start.9 = (f32[4,128,128]{2,1,0:T(8,128)S(1)}, f32[4,128,128]{2,1,0:T(8,128)S(1)}, u32[]{:S(2)}, u32[]{:S(2)}) collective-permute-start(f32[4,128,128]{2,1,0:T(8,128)S(1)} %convolution_select_fusion), channel_id=1, source_target_pairs={{0,4},{4,0},{8,12},{12,8},{16,20},{20,16},{24,28},{28,24},{32,36},... | collective-permute-start | bytes 786440 | tf_op jit(solution)/shard_map/ppermute | solution.py:68
  125.1 1.9 %convolution_subtract_fusion = f32[8,256,128]{2,1,0:T(8,128)S(1)} fusion(f32[8,128,128]{2,1,0:T(8,128)S(1)} %multiply_bitcast_fusion, f32[8,128,384]{2,1,0:T(8,128)S(1)} %fusion.8, bf16[128,8,128]{2,0,1:T(8,128)(2,1)S(1)} %copy-done.2, bf16[128,8,128]{2,0,1:T(8,128)(2,1)S(1)} %copy-done.4), kind=kOutput, calls=%fused_computation.12 | convolution fusion | flops 404226048 | bytes 3145728 | tf_op jit(solution)/shard_map/hit,hid->htd/dot_general | solution.py:167
  (125 shorter events, 31.7 us)
Async XLA Ops:
  0.6 7.2 %copy-start = (bf16[128,1024]{1,0:T(8,128)(2,1)S(1)}, bf16[128,1024]{1,0:T(8,128)(2,1)}, u32[]{:S(2)}) copy-start(bf16[128,1024]{1,0:T(8,128)(2,1)} %param.6) | copy-start | bytes 786436
  0.6 14.4 %collective-permute-start.2 = (bf16[128,1024]{1,0:T(8,128)(2,1)}, bf16[128,1024]{1,0:T(8,128)(2,1)S(1)}, u32[]{:S(2)}, u32[]{:S(2)}) collective-permute-start(bf16[128,1024]{1,0:T(8,128)(2,1)} %param.4), channel_id=1, source_target_pairs={{0,3},{1,0},{2,1},{3,2},{4,7},{5,4},{6,5},{7,6},{8,11},{9,8},{10,9... | collective-permute-start | bytes 786440 | tf_op jit(solution)/shard_map/ppermute | solution.py:84
  4.3 13.1 %collective-permute-start.1 = (bf16[128,1024]{1,0:T(8,128)(2,1)}, bf16[128,1024]{1,0:T(8,128)(2,1)S(1)}, u32[]{:S(2)}, u32[]{:S(2)}) collective-permute-start(bf16[128,1024]{1,0:T(8,128)(2,1)} %param.4), channel_id=1, source_target_pairs={{0,2},{1,3},{2,0},{3,1},{4,6},{5,7},{6,4},{7,5},{8,10},{9,11},{10,... | collective-permute-start | bytes 786440 | tf_op jit(solution)/shard_map/ppermute | solution.py:84
  4.6 15.3 %collective-permute-start = (bf16[128,1024]{1,0:T(8,128)(2,1)}, bf16[128,1024]{1,0:T(8,128)(2,1)}, u32[]{:S(2)}, u32[]{:S(2)}) collective-permute-start(bf16[128,1024]{1,0:T(8,128)(2,1)} %param.4), channel_id=1, source_target_pairs={{0,1},{1,2},{2,3},{3,0},{4,5},{5,6},{6,7},{7,4},{8,9},{9,10},{10,1... | collective-permute-start | bytes 786440 | tf_op jit(solution)/shard_map/ppermute | solution.py:84
  5.4 2.4 %copy-start.11 = (bf16[128,1024]{1,0:T(8,128)(2,1)S(1)}, bf16[128,1024]{1,0:T(8,128)(2,1)}, u32[]{:S(2)}) copy-start(bf16[128,1024]{1,0:T(8,128)(2,1)} %param.7) | copy-start | bytes 786436
  7.9 31.1 %copy-start.1 = (bf16[128,8,128]{2,0,1:T(8,128)(2,1)}, bf16[128,8,128]{2,0,1:T(8,128)(2,1)S(1)}, u32[]{:S(2)}) copy-start(bf16[128,8,128]{2,0,1:T(8,128)(2,1)S(1)} %get-tuple-element.12) | copy-start | bytes 786436
  7.9 31.1 %copy-start.3 = (bf16[128,8,128]{2,0,1:T(8,128)(2,1)}, bf16[128,8,128]{2,0,1:T(8,128)(2,1)S(1)}, u32[]{:S(2)}) copy-start(bf16[128,8,128]{2,0,1:T(8,128)(2,1)S(1)} %get-tuple-element.13) | copy-start | bytes 786436
  42.4 3.1 %collective-permute-start.3 = (f32[8,128,128]{2,1,0:T(8,128)S(1)}, f32[8,128,128]{2,1,0:T(8,128)S(1)}, u32[]{:S(2)}, u32[]{:S(2)}) collective-permute-start(f32[8,128,128]{2,1,0:T(8,128)S(1)} %convolution_subtract_fusion.1), channel_id=1, source_target_pairs={{0,4},{4,0},{8,12},{12,8},{16,20},{20,16},{24,28},{28,24},{32,36},... | collective-permute-start | bytes 1572872 | tf_op jit(solution)/shard_map/ppermute | solution.py:43
  46.2 3.2 %copy-start.10 = (f32[4,128,128]{2,1,0:T(8,128)}, f32[4,128,128]{2,1,0:T(8,128)S(1)}, u32[]{:S(2)}) copy-start(f32[4,128,128]{2,1,0:T(8,128)S(1)} %constant_dynamic-slice_fusion) | copy-start | bytes 786436
  46.2 8.4 %collective-permute-start.4 = (f32[4,128,128]{2,1,0:T(8,128)S(1)}, f32[4,128,128]{2,1,0:T(8,128)S(1)}, u32[]{:S(2)}, u32[]{:S(2)}) collective-permute-start(f32[4,128,128]{2,1,0:T(8,128)S(1)} %constant_dynamic-slice_fusion), channel_id=1, source_target_pairs={{0,8},{4,12},{8,16},{12,20},{16,24},{20,28},{24,32},{28,36},{32,40... | collective-permute-start | bytes 786440 | tf_op jit(solution)/shard_map/ppermute | solution.py:53
  54.6 11.6 %copy-start.8 = (f32[4,128,128]{2,1,0:T(8,128)}, f32[4,128,128]{2,1,0:T(8,128)S(1)}, u32[]{:S(2)}) copy-start(f32[4,128,128]{2,1,0:T(8,128)S(1)} %collective-permute-done.4) | copy-start | bytes 786436
  56.1 10.1 %copy-start.7 = (f32[4,128,128]{2,1,0:T(8,128)}, f32[4,128,128]{2,1,0:T(8,128)S(1)}, u32[]{:S(2)}) copy-start(f32[4,128,128]{2,1,0:T(8,128)S(1)} %convolution_select_fusion.1) | copy-start | bytes 786436
  56.1 10.1 %collective-permute-start.5 = (f32[4,128,128]{2,1,0:T(8,128)S(1)}, f32[4,128,128]{2,1,0:T(8,128)}, u32[]{:S(2)}, u32[]{:S(2)}) collective-permute-start(f32[4,128,128]{2,1,0:T(8,128)S(1)} %convolution_select_fusion.1), channel_id=1, source_target_pairs={{0,16},{4,20},{8,24},{12,28},{16,32},{20,36},{24,40},{28,44},{32,4... | collective-permute-start | bytes 786440 | tf_op jit(solution)/shard_map/ppermute | solution.py:53
  68.7 11.2 %copy-start.5 = (f32[4,128,128]{2,1,0:T(8,128)}, f32[4,128,128]{2,1,0:T(8,128)S(1)}, u32[]{:S(2)}) copy-start(f32[4,128,128]{2,1,0:T(8,128)S(1)} %get-tuple-element.8) | copy-start | bytes 786436
  68.8 11.2 %copy-start.6 = (f32[4,128,128]{2,1,0:T(8,128)}, f32[4,128,128]{2,1,0:T(8,128)S(1)}, u32[]{:S(2)}) copy-start(f32[4,128,128]{2,1,0:T(8,128)S(1)} %get-tuple-element.9) | copy-start | bytes 786436
  68.8 11.2 %collective-permute-start.6 = (f32[4,128,128]{2,1,0:T(8,128)S(1)}, f32[4,128,128]{2,1,0:T(8,128)}, u32[]{:S(2)}, u32[]{:S(2)}) collective-permute-start(f32[4,128,128]{2,1,0:T(8,128)S(1)} %get-tuple-element.9), channel_id=1, source_target_pairs={{0,32},{4,36},{8,40},{12,44},{16,48},{20,52},{24,56},{28,60},{32,6... | collective-permute-start | bytes 786440 | tf_op jit(solution)/shard_map/ppermute | solution.py:53
  81.5 43.6 %copy-start.2 = (bf16[128,8,128]{2,0,1:T(8,128)(2,1)S(1)}, bf16[128,8,128]{2,0,1:T(8,128)(2,1)}, u32[]{:S(2)}) copy-start(bf16[128,8,128]{2,0,1:T(8,128)(2,1)} %copy-done.1) | copy-start | bytes 786436
  81.5 43.6 %copy-start.4 = (bf16[128,8,128]{2,0,1:T(8,128)(2,1)S(1)}, bf16[128,8,128]{2,0,1:T(8,128)(2,1)}, u32[]{:S(2)}) copy-start(bf16[128,8,128]{2,0,1:T(8,128)(2,1)} %copy-done.3) | copy-start | bytes 786436
  83.5 8.1 %collective-permute-start.7 = (f32[4,128,128]{2,1,0:T(8,128)}, f32[4,128,128]{2,1,0:T(8,128)}, u32[]{:S(2)}, u32[]{:S(2)}) collective-permute-start(f32[4,128,128]{2,1,0:T(8,128)} %get-tuple-element.7), channel_id=1, source_target_pairs={{0,64},{4,68},{8,72},{12,76},{16,80},{20,84},{24,88},{28,92},{32,9... | collective-permute-start | bytes 786440 | tf_op jit(solution)/shard_map/ppermute | solution.py:53
  93.3 0.8 copy-start.9
  95.8 25.4 %collective-permute-start.8 = (f32[4,128,128]{2,1,0:T(8,128)}, f32[4,128,128]{2,1,0:T(8,128)}, u32[]{:S(2)}, u32[]{:S(2)}) collective-permute-start(f32[4,128,128]{2,1,0:T(8,128)} %slice_select_fusion.2), channel_id=1, source_target_pairs={{0,128},{4,132},{8,136},{12,140},{16,144},{20,148},{24,152},{28,15... | collective-permute-start | bytes 786440 | tf_op jit(solution)/shard_map/ppermute | solution.py:53
  122.9 4.2 %collective-permute-start.9 = (f32[4,128,128]{2,1,0:T(8,128)S(1)}, f32[4,128,128]{2,1,0:T(8,128)S(1)}, u32[]{:S(2)}, u32[]{:S(2)}) collective-permute-start(f32[4,128,128]{2,1,0:T(8,128)S(1)} %convolution_select_fusion), channel_id=1, source_target_pairs={{0,4},{4,0},{8,12},{12,8},{16,20},{20,16},{24,28},{28,24},{32,36},... | collective-permute-start | bytes 786440 | tf_op jit(solution)/shard_map/ppermute | solution.py:68

commit v3 on v2

--- a/solution.py
+++ b/solution.py
@@ -74,6 +74,64 @@
     return combine(full, inner)
 
 
+def strided_scan(array, axis, count, stride, combine, start):
+    place = lax.axis_index(axis)
+    span = array
+    before = start
+    shift = stride
+    while shift < count:
+        pairs = [(k, k + shift) for k in range(count - shift)]
+        arrived = lax.ppermute(span, axis, pairs)
+        reached = place >= shift
+        last = shift * 2 >= count
+        if shift == stride:
+            before = jnp.where(reached, arrived, start)
+            if not last:
+                span = jnp.where(reached, combine(arrived, span), span)
+        elif last:
+            before = jnp.where(reached, combine(arrived, before), before)
+        else:
+            width = array.shape[-1]
+            both = combine(arrived, jnp.concatenate([span, before], axis=-1))
+            span = jnp.where(reached, both[..., :width], span)
+            before = jnp.where(reached, both[..., width:], before)
+        shift = shift * 2
+    return before
+
+
+def row_exchange(pieces, axis, count, row):
+    place = lax.axis_index(axis)
+    pos = place % row
+    got = [pieces(pos)]
+    for step in range(1, row):
+        pairs = [(k, (k // row) * row + (k % row + step) % row) for k in range(count)]
+        got.append(lax.ppermute(pieces((pos + step) % row), axis, pairs))
+    order = (pos + row - jnp.arange(row)) % row
+    return jnp.take(jnp.stack(got), order, axis=0)
+
+
+def row_entering(array, axis, count, row, combine, identity):
+    place = lax.axis_index(axis)
+    heads, size = array.shape[0], array.shape[-1]
+    share = heads // row
+    eye = jnp.broadcast_to(identity, (share, size, size))
+    blocks = row_exchange(
+        lambda g: lax.dynamic_slice_in_dim(array, g * share, share, 0), axis, count, row
+    )
+    prefix = [eye]
+    for q in range(1, row):
+        prefix.append(combine(prefix[-1], blocks[q - 1]))
+    whole = combine(prefix[-1], blocks[row - 1])
+    outer = strided_scan(whole, axis, count, row, combine, eye)
+    spread = jnp.broadcast_to(outer[None], (row, share, size, size)).reshape(row * share, size, size)
+    carried = combine(spread, jnp.stack(prefix).reshape(row * share, size, size))
+    carried = carried.reshape(row, share, size, size)
+    full = row_exchange(
+        lambda q: lax.dynamic_index_in_dim(carried, q, 0, keepdims=False), axis, count, row
+    )
+    return full.reshape(heads, size, size)
+
+
 def gathered_projection(features, proj_weight, axis, count):
     place = lax.axis_index(axis)
     width = features.shape[1]
@@ -173,7 +231,10 @@
     def combine(earlier, later):
         return jnp.einsum("hde,hef->hdf", earlier, later, precision=highest)
 
-    if seq_count % 2 == 0 and local_heads % 2 == 0:
+    row = 8
+    if seq_count % row == 0 and seq_count > row and local_heads % row == 0:
+        carried = row_entering(block_product, "seq", seq_count, row, combine, identity[0])
+    elif seq_count % 2 == 0 and local_heads % 2 == 0:
         carried = paired_entering(block_product, "seq", seq_count, combine, identity[0])
     else:
         carried = entering(block_product, "seq", seq_count, combine, identity)

time: 133 us -> 106 us (0.80); the launches traced: 131 us -> 105 us
  waiting for transfers between devices: 27.6 us -> 11.9 us
  starting transfers between devices: 52.7 us -> 44.8 us
  local copies, waits for them, and re-layouts: 3.29 us -> 9.91 us
  other arithmetic: 5.33 us -> 0.79 us
  matrix products: 40.2 us -> 36.2 us
    ppermute x7 -> x17, waiting for transfers between devices: 20.4 us -> 6.52 us  [the longest x14 3.81 us: row_exchange(): got.append(lax.ppermute(pieces((pos + step) % row), axis, pairs))]
    ppermute x7 -> x17, starting transfers between devices: 48 us -> 39.5 us  [the longest x3 20 us: strided_scan(): arrived = lax.ppermute(span, axis, pairs)]
    dot_general x7 -> x12, matrix products: 9.27 us -> 3.99 us  [combine(): return jnp.einsum('hde,hef->hdf', earlier, later, precision=highest)]
    select_n x4, other arithmetic: 4.72 us -> 0.14 us  [the longest x2 0.12 us: row_exchange(): return jnp.take(jnp.stack(got), order, axis=0)]
    unnamed x26, local copies, waits for them, and re-layouts: 2.56 us -> 6.2 us
    gather x0 -> x2, local copies, waits for them, and re-layouts: none -> 2.2 us  [row_exchange(): return jnp.take(jnp.stack(got), order, axis=0)]
    ppermute x3, waiting for transfers between devices: 7.22 us -> 5.34 us  [gathered_projection(): part = lax.ppermute(features, axis, pairs)]
  transfers between devices with their start and end apart: 10 -> 20, of which waited for: 8 -> 8; matrix products, arithmetic and copies ran while one was open for 7% -> 14% of each run, Pallas kernels for 0% -> 0%
where the time goes in v3:
time: 106 us; the launch traced here: 105 us
  starting transfers between devices  44.8 us (42%)
  matrix products  36.2 us (34%)
  waiting for transfers between devices  11.9 us (11%)
  local copies, waits for them, and re-layouts  9.91 us (9%)
  between operations  1.78 us (2%)
    ppermute x3, starting transfers between devices, strided_scan(): arrived = lax.ppermute(span, axis, pairs)  20 us
    ppermute x14, starting transfers between devices, row_exchange(): got.append(lax.ppermute(pieces((pos + step) % row), axis, pairs))  19.5 us
    dot_general x3, matrix products, gathered_projection(): jnp.dot(part, rows(owner), preferred_element_type=jnp.float32)  7.06 us
    unnamed x26, local copies, waits for them, and re-layouts  6.2 us
    ppermute x3, waiting for transfers between devices, gathered_projection(): part = lax.ppermute(features, axis, pairs)  5.34 us
    ppermute x3, starting transfers between devices, gathered_projection(): part = lax.ppermute(features, axis, pairs)  5.28 us
    dot_general x24, matrix products, small_inverse(): power = jnp.einsum('hij,hjk->hik', power, power, precision=highest)  5.08 us
    dot_general x24, matrix products, small_inverse(): jnp.einsum('hij,hjk->hik', result, power, precision=highest)  5.06 us
  transfers between devices with their start and end apart: 20, of which 8 were waited for; matrix products, arithmetic and copies ran while one was open for 14% of the time, Pallas kernels for 0%

profile of v3, /device:TPU:1, one launch (start us, length us, event | category | flops | bytes accessed | tf_op | source)
XLA Modules:
  0.0 105.3 jit_solution(2730228493251812454)
XLA Ops:
  0.6 3.8 %collective-permute-start.1 = (bf16[128,1024]{1,0:T(8,128)(2,1)}, bf16[128,1024]{1,0:T(8,128)(2,1)S(1)}, u32[]{:S(2)}, u32[]{:S(2)}) collective-permute-start(bf16[128,1024]{1,0:T(8,128)(2,1)} %param.6), channel_id=1, source_target_pairs={{0,2},{1,3},{2,0},{3,1},{4,6},{5,7},{6,4},{7,5},{8,10},{9,11},{10,... | collective-permute-start | bytes 786440 | tf_op jit(solution)/shard_map/ppermute | solution.py:142
  6.1 2.4 %fusion.6 = f32[1024,128]{1,0:T(8,128)S(1)} fusion(bf16[128,1024]{1,0:T(8,128)(2,1)} %param.6, bf16[4096,1024]{1,0:T(8,128)(2,1)} %param.7, s32[]{:T(128)S(6)} %select_n.164), kind=kOutput, calls=%fused_computation.8 | convolution fusion | flops 268435456 | bytes 2883588 | tf_op jit(solution)/shard_map/dot_general | solution.py:139
  9.8 2.3 %fusion.2 = f32[1024,128]{1,0:T(8,128)S(1)} fusion(bf16[128,1024]{1,0:T(8,128)(2,1)S(1)} %collective-permute-done.1, bf16[4096,1024]{1,0:T(8,128)(2,1)} %param.7, s32[]{:T(128)S(6)} %select_n.168), kind=kOutput, calls=%fused_computation.4 | convolution fusion | flops 268435456 | bytes 2883588 | tf_op jit(solution)/shard_map/dot_general | solution.py:144
  12.2 4.4 %collective-permute-done.2 = bf16[128,1024]{1,0:T(8,128)(2,1)S(1)} collective-permute-done((bf16[128,1024]{1,0:T(8,128)(2,1)}, bf16[128,1024]{1,0:T(8,128)(2,1)S(1)}, u32[]{:S(2)}, u32[]{:S(2)}) %collective-permute-start.2) | collective-permute-done | bytes 262176 | tf_op jit(solution)/shard_map/ppermute | solution.py:142
  16.6 2.3 %fusion = f32[1024,128]{1,0:T(8,128)S(1)} fusion(bf16[128,1024]{1,0:T(8,128)(2,1)S(1)} %collective-permute-done.2, bf16[4096,1024]{1,0:T(8,128)(2,1)} %param.7, s32[]{:T(128)S(6)} %select_n.170), kind=kOutput, calls=%fused_computation.2 | convolution fusion | flops 268435456 | bytes 2883588 | tf_op jit(solution)/shard_map/dot_general | solution.py:144
  18.9 2.4 %multiply_reduce_fusion = (f32[128,8]{0,1:T(8,128)S(1)}, f32[1024,128]{1,0:T(8,128)S(1)}) fusion(f32[1024,128]{1,0:T(8,128)S(1)} %fusion, f32[1024,128]{1,0:T(8,128)S(1)} %fusion.2, f32[1024,128]{1,0:T(8,128)S(1)} %fusion.6, bf16[128,1024]{1,0:T(8,128)(2,1)} %collective-permute-done, bf16[4096,1024]{1,0:T(8,128)(2,1)} %param.7, s32[]{:T(128)S(6)} %select_n.166), kind=kOutput, calls=%fused_computation.92 | convolution fusion | flops 269089792 | bytes 4460548 | tf_op jit(solution)/shard_map/dot_general | solution.py:144
  21.7 1.2 %fusion.16 = f32[8,128,128]{2,1,0:T(8,128)S(1)} fusion(f32[8,128,128]{2,1,0:T(8,128)S(1)} %multiply_bitcast_fusion, f32[128,128]{1,0:T(8,128)S(1)} %fusion.115, f32[128,128]{1,0:T(8,128)S(1)} %fusion.116), kind=kOutput, calls=%fused_computation.21 | convolution fusion | flops 201588736 | bytes 1179648 | tf_op jit(solution)/shard_map/hid,hjd->hij/dot_general | solution.py:212
  38.9 1.5 %fusion.8 = f32[8,128,384]{2,1,0:T(8,128)S(1)} fusion(f32[8,128,128]{2,1,0:T(8,128)S(1)} %multiply_bitcast_fusion, f32[8,128,256]{2,1,0:T(8,128)S(1)} %convolution_multiply_fusion, f32[8,64,64]{2,1,0:T(8,128)S(1)} %select_maximum_fusion.2, f32[8,64,64]{2,1,0:T(8,128)S(1)} %convolution_negate_fusion, f32[8,32,64]{2,1,0:T(8,128)S(1)} %concatenate.83, ...), kind=kOutput, calls=%fused_computation.10 | convolution fusion | flops 605421568 | bytes 3538944 | tf_op jit(solution)/shard_map/hij,hjk->hik/dot_general | solution.py:190
  41.5 2.5 %collective-permute-start.3 = (f32[1,128,128]{2,1,0:T(8,128)S(1)}, f32[1,128,128]{2,1,0:T(8,128)S(1)}, u32[]{:S(2)}, u32[]{:S(2)}) collective-permute-start(f32[1,128,128]{2,1,0:T(8,128)S(1)} %get-tuple-element.20), channel_id=1, source_target_pairs={{0,4},{4,8},{8,12},{12,16},{16,20},{20,24},{24,28},{28,0},{32,36},... | collective-permute-start | bytes 196616 | tf_op jit(solution)/shard_map/ppermute | solution.py:108
  45.3 1.6 %collective-permute-start.5 = (f32[1,128,128]{2,1,0:T(8,128)S(1)}, f32[1,128,128]{2,1,0:T(8,128)S(1)}, u32[]{:S(2)}, u32[]{:S(2)}) collective-permute-start(f32[1,128,128]{2,1,0:T(8,128)S(1)} %get-tuple-element.18), channel_id=1, source_target_pairs={{0,12},{4,16},{8,20},{12,24},{16,28},{20,0},{24,4},{28,8},{32,44},... | collective-permute-start | bytes 196616 | tf_op jit(solution)/shard_map/ppermute | solution.py:108
  47.4 1.9 %collective-permute-start.7 = (f32[1,128,128]{2,1,0:T(8,128)S(1)}, f32[1,128,128]{2,1,0:T(8,128)S(1)}, u32[]{:S(2)}, u32[]{:S(2)}) collective-permute-start(f32[1,128,128]{2,1,0:T(8,128)S(1)} %get-tuple-element.16), channel_id=1, source_target_pairs={{0,20},{4,24},{8,28},{12,0},{16,4},{20,8},{24,12},{28,16},{32,52},... | collective-permute-start | bytes 196616 | tf_op jit(solution)/shard_map/ppermute | solution.py:108
  51.3 1.7 %collective-permute-start.9 = (f32[1,128,128]{2,1,0:T(8,128)S(1)}, f32[1,128,128]{2,1,0:T(8,128)S(1)}, u32[]{:S(2)}, u32[]{:S(2)}) collective-permute-start(f32[1,128,128]{2,1,0:T(8,128)S(1)} %get-tuple-element.14), channel_id=1, source_target_pairs={{0,28},{4,0},{8,4},{12,8},{16,12},{20,16},{24,20},{28,24},{32,60},... | collective-permute-start | bytes 196616 | tf_op jit(solution)/shard_map/ppermute | solution.py:108
  56.7 1.6 %gather_fusion = f32[8,128,128]{2,1,0:T(8,128)S(1)} fusion(f32[8,128,128]{2,1,0:T(8,128)} %bitcast.13, s32[1024]{0:T(1024)S(1)} %pad_clamp_fusion), kind=kCustom, calls=%fused_computation.clone | custom fusion | bytes 1048608 | tf_op jit(solution)/shard_map/jit(_take)/gather | solution.py:110
  60.3 3.5 %collective-permute-start.10 = (f32[1,128,128]{1,2,0:T(8,128)S(1)}, f32[1,128,128]{1,2,0:T(8,128)S(1)}, u32[]{:S(2)}, u32[]{:S(2)}) collective-permute-start(f32[1,128,128]{1,2,0:T(8,128)S(1)} %bitcast.264), channel_id=1, source_target_pairs={{0,32},{4,36},{8,40},{12,44},{16,48},{20,52},{24,56},{28,60},{32,6... | collective-permute-start | bytes 196616 | tf_op jit(solution)/shard_map/ppermute | solution.py:84
  63.8 1.4 %collective-permute-done.10 = f32[1,128,128]{1,2,0:T(8,128)S(1)} collective-permute-done((f32[1,128,128]{1,2,0:T(8,128)S(1)}, f32[1,128,128]{1,2,0:T(8,128)S(1)}, u32[]{:S(2)}, u32[]{:S(2)}) %collective-permute-start.10) | collective-permute-done | bytes 65568 | tf_op jit(solution)/shard_map/ppermute | solution.py:84
  65.4 5.5 %collective-permute-start.11 = (f32[1,128,128]{1,2,0:T(8,128)S(1)}, f32[1,128,128]{1,2,0:T(8,128)S(1)}, u32[]{:S(2)}, u32[]{:S(2)}) collective-permute-start(f32[1,128,128]{1,2,0:T(8,128)S(1)} %fusion.31), channel_id=1, source_target_pairs={{0,64},{4,68},{8,72},{12,76},{16,80},{20,84},{24,88},{28,92},{32,9... | collective-permute-start | bytes 196616 | tf_op jit(solution)/shard_map/ppermute | solution.py:84
  70.9 1.3 %collective-permute-done.11 = f32[1,128,128]{1,2,0:T(8,128)S(1)} collective-permute-done((f32[1,128,128]{1,2,0:T(8,128)S(1)}, f32[1,128,128]{1,2,0:T(8,128)S(1)}, u32[]{:S(2)}, u32[]{:S(2)}) %collective-permute-start.11) | collective-permute-done | bytes 65568 | tf_op jit(solution)/shard_map/ppermute | solution.py:84
  72.5 11.0 %collective-permute-start.12 = (f32[1,128,128]{1,2,0:T(8,128)S(1)}, f32[1,128,128]{1,2,0:T(8,128)S(1)}, u32[]{:S(2)}, u32[]{:S(2)}) collective-permute-start(f32[1,128,128]{1,2,0:T(8,128)S(1)} %slice_select_fusion.1), channel_id=1, source_target_pairs={{0,128},{4,132},{8,136},{12,140},{16,144},{20,148},{24,152},{28,15... | collective-permute-start | bytes 196616 | tf_op jit(solution)/shard_map/ppermute | solution.py:84
  83.6 3.0 %convolution_subtract_fusion = f32[8,256,128]{2,1,0:T(8,128)S(1)} fusion(f32[8,128,128]{2,1,0:T(8,128)S(1)} %multiply_bitcast_fusion, f32[8,128,384]{2,1,0:T(8,128)S(1)} %fusion.8, bf16[128,8,128]{2,0,1:T(8,128)(2,1)} %copy-done.1, bf16[128,8,128]{2,0,1:T(8,128)(2,1)} %copy-done.2), kind=kOutput, calls=%fused_computation.14 | convolution fusion | flops 404226048 | bytes 3145728 | tf_op jit(solution)/shard_map/hit,hid->htd/dot_general | solution.py:225
  86.9 1.6 %fusion.49 = f32[8,128,128]{2,1,0:T(8,128)S(1)} fusion(f32[8,1,128,128]{3,2,1,0:T(8,128)} %copy-done.3, f32[128,128]{1,0:T(8,128)S(1)} %copy.12), kind=kOutput, calls=%fused_computation.88 | convolution fusion | flops 201326592 | bytes 1114112 | tf_op jit(solution)/shard_map/hde,hef->hdf/dot_general | solution.py:232
  88.6 2.4 %collective-permute-start.13 = (f32[1,128,128]{2,1,0:T(8,128)S(1)}, f32[1,128,128]{2,1,0:T(8,128)S(1)}, u32[]{:S(2)}, u32[]{:S(2)}) collective-permute-start(f32[1,128,128]{2,1,0:T(8,128)S(1)} %get-tuple-element.13), channel_id=1, source_target_pairs={{0,4},{4,8},{8,12},{12,16},{16,20},{20,24},{24,28},{28,0},{32,36},... | collective-permute-start | bytes 196616 | tf_op jit(solution)/shard_map/ppermute | solution.py:108
  91.4 2.6 %collective-permute-start.15 = (f32[1,128,128]{2,1,0:T(8,128)S(1)}, f32[1,128,128]{2,1,0:T(8,128)S(1)}, u32[]{:S(2)}, u32[]{:S(2)}) collective-permute-start(f32[1,128,128]{2,1,0:T(8,128)S(1)} %get-tuple-element.11), channel_id=1, source_target_pairs={{0,12},{4,16},{8,20},{12,24},{16,28},{20,0},{24,4},{28,8},{32,44},... | collective-permute-start | bytes 196616 | tf_op jit(solution)/shard_map/ppermute | solution.py:108
  94.5 2.6 %collective-permute-start.17 = (f32[1,128,128]{2,1,0:T(8,128)S(1)}, f32[1,128,128]{2,1,0:T(8,128)S(1)}, u32[]{:S(2)}, u32[]{:S(2)}) collective-permute-start(f32[1,128,128]{2,1,0:T(8,128)S(1)} %get-tuple-element.9), channel_id=1, source_target_pairs={{0,20},{4,24},{8,28},{12,0},{16,4},{20,8},{24,12},{28,16},{32,52},... | collective-permute-start | bytes 196616 | tf_op jit(solution)/shard_map/ppermute | solution.py:108
  97.9 1.8 %collective-permute-done.16 = f32[1,128,128]{2,1,0:T(8,128)S(1)} collective-permute-done((f32[1,128,128]{2,1,0:T(8,128)S(1)}, f32[1,128,128]{2,1,0:T(8,128)S(1)}, u32[]{:S(2)}, u32[]{:S(2)}) %collective-permute-start.16) | collective-permute-done | bytes 65568 | tf_op jit(solution)/shard_map/ppermute | solution.py:108
  (159 shorter events, 36.9 us)
Async XLA Ops:
  0.6 7.9 %copy-start = (bf16[128,1024]{1,0:T(8,128)(2,1)S(1)}, bf16[128,1024]{1,0:T(8,128)(2,1)}, u32[]{:S(2)}) copy-start(bf16[128,1024]{1,0:T(8,128)(2,1)} %param.8) | copy-start | bytes 786436
  0.6 9.2 %collective-permute-start.1 = (bf16[128,1024]{1,0:T(8,128)(2,1)}, bf16[128,1024]{1,0:T(8,128)(2,1)S(1)}, u32[]{:S(2)}, u32[]{:S(2)}) collective-permute-start(bf16[128,1024]{1,0:T(8,128)(2,1)} %param.6), channel_id=1, source_target_pairs={{0,2},{1,3},{2,0},{3,1},{4,6},{5,7},{6,4},{7,5},{8,10},{9,11},{10,... | collective-permute-start | bytes 786440 | tf_op jit(solution)/shard_map/ppermute | solution.py:142
  4.5 12.1 %collective-permute-start.2 = (bf16[128,1024]{1,0:T(8,128)(2,1)}, bf16[128,1024]{1,0:T(8,128)(2,1)S(1)}, u32[]{:S(2)}, u32[]{:S(2)}) collective-permute-start(bf16[128,1024]{1,0:T(8,128)(2,1)} %param.6), channel_id=1, source_target_pairs={{0,3},{1,0},{2,1},{3,2},{4,7},{5,4},{6,5},{7,6},{8,11},{9,8},{10,9... | collective-permute-start | bytes 786440 | tf_op jit(solution)/shard_map/ppermute | solution.py:142
  5.2 13.7 %collective-permute-start = (bf16[128,1024]{1,0:T(8,128)(2,1)}, bf16[128,1024]{1,0:T(8,128)(2,1)}, u32[]{:S(2)}, u32[]{:S(2)}) collective-permute-start(bf16[128,1024]{1,0:T(8,128)(2,1)} %param.6), channel_id=1, source_target_pairs={{0,1},{1,2},{2,3},{3,0},{4,5},{5,6},{6,7},{7,4},{8,9},{9,10},{10,1... | collective-permute-start | bytes 786440 | tf_op jit(solution)/shard_map/ppermute | solution.py:142
  8.6 29.6 %copy-start.1 = (bf16[128,8,128]{2,0,1:T(8,128)(2,1)}, bf16[128,8,128]{2,0,1:T(8,128)(2,1)S(1)}, u32[]{:S(2)}) copy-start(bf16[128,8,128]{2,0,1:T(8,128)(2,1)S(1)} %get-tuple-element.37) | copy-start | bytes 786436
  8.6 29.6 %copy-start.2 = (bf16[128,8,128]{2,0,1:T(8,128)(2,1)}, bf16[128,8,128]{2,0,1:T(8,128)(2,1)S(1)}, u32[]{:S(2)}) copy-start(bf16[128,8,128]{2,0,1:T(8,128)(2,1)S(1)} %get-tuple-element.38) | copy-start | bytes 786436
  41.5 8.4 %collective-permute-start.3 = (f32[1,128,128]{2,1,0:T(8,128)S(1)}, f32[1,128,128]{2,1,0:T(8,128)S(1)}, u32[]{:S(2)}, u32[]{:S(2)}) collective-permute-start(f32[1,128,128]{2,1,0:T(8,128)S(1)} %get-tuple-element.20), channel_id=1, source_target_pairs={{0,4},{4,8},{8,12},{12,16},{16,20},{20,24},{24,28},{28,0},{32,36},... | collective-permute-start | bytes 196616 | tf_op jit(solution)/shard_map/ppermute | solution.py:108
  44.1 7.2 %collective-permute-start.4 = (f32[1,128,128]{2,1,0:T(8,128)S(1)}, f32[1,128,128]{2,1,0:T(8,128)S(1)}, u32[]{:S(2)}, u32[]{:S(2)}) collective-permute-start(f32[1,128,128]{2,1,0:T(8,128)S(1)} %get-tuple-element.19), channel_id=1, source_target_pairs={{0,8},{4,12},{8,16},{12,20},{16,24},{20,28},{24,0},{28,4},{32,40},... | collective-permute-start | bytes 196616 | tf_op jit(solution)/shard_map/ppermute | solution.py:108
  45.3 8.3 %collective-permute-start.5 = (f32[1,128,128]{2,1,0:T(8,128)S(1)}, f32[1,128,128]{2,1,0:T(8,128)S(1)}, u32[]{:S(2)}, u32[]{:S(2)}) collective-permute-start(f32[1,128,128]{2,1,0:T(8,128)S(1)} %get-tuple-element.18), channel_id=1, source_target_pairs={{0,12},{4,16},{8,20},{12,24},{16,28},{20,0},{24,4},{28,8},{32,44},... | collective-permute-start | bytes 196616 | tf_op jit(solution)/shard_map/ppermute | solution.py:108
  46.9 7.3 %collective-permute-start.6 = (f32[1,128,128]{2,1,0:T(8,128)S(1)}, f32[1,128,128]{2,1,0:T(8,128)S(1)}, u32[]{:S(2)}, u32[]{:S(2)}) collective-permute-start(f32[1,128,128]{2,1,0:T(8,128)S(1)} %get-tuple-element.17), channel_id=1, source_target_pairs={{0,16},{4,20},{8,24},{12,28},{16,0},{20,4},{24,8},{28,12},{32,48},... | collective-permute-start | bytes 196616 | tf_op jit(solution)/shard_map/ppermute | solution.py:108
  47.4 7.5 %collective-permute-start.7 = (f32[1,128,128]{2,1,0:T(8,128)S(1)}, f32[1,128,128]{2,1,0:T(8,128)S(1)}, u32[]{:S(2)}, u32[]{:S(2)}) collective-permute-start(f32[1,128,128]{2,1,0:T(8,128)S(1)} %get-tuple-element.16), channel_id=1, source_target_pairs={{0,20},{4,24},{8,28},{12,0},{16,4},{20,8},{24,12},{28,16},{32,52},... | collective-permute-start | bytes 196616 | tf_op jit(solution)/shard_map/ppermute | solution.py:108
  50.0 5.5 %collective-permute-start.8 = (f32[1,128,128]{2,1,0:T(8,128)S(1)}, f32[1,128,128]{2,1,0:T(8,128)S(1)}, u32[]{:S(2)}, u32[]{:S(2)}) collective-permute-start(f32[1,128,128]{2,1,0:T(8,128)S(1)} %get-tuple-element.15), channel_id=1, source_target_pairs={{0,24},{4,28},{8,0},{12,4},{16,8},{20,12},{24,16},{28,20},{32,56},... | collective-permute-start | bytes 196616 | tf_op jit(solution)/shard_map/ppermute | solution.py:108
  51.3 4.9 %collective-permute-start.9 = (f32[1,128,128]{2,1,0:T(8,128)S(1)}, f32[1,128,128]{2,1,0:T(8,128)S(1)}, u32[]{:S(2)}, u32[]{:S(2)}) collective-permute-start(f32[1,128,128]{2,1,0:T(8,128)S(1)} %get-tuple-element.14), channel_id=1, source_target_pairs={{0,28},{4,0},{8,4},{12,8},{16,12},{20,16},{24,20},{28,24},{32,60},... | collective-permute-start | bytes 196616 | tf_op jit(solution)/shard_map/ppermute | solution.py:108
  59.9 12.6 %copy-start.3 = (f32[8,1,128,128]{3,2,1,0:T(8,128)}, f32[8,1,128,128]{3,2,1,0:T(8,128)S(1)}, u32[]{:S(2)}) copy-start(f32[8,1,128,128]{3,2,1,0:T(8,128)S(1)} %get-tuple-element.35) | copy-start | bytes 1572868
  60.3 5.0 %collective-permute-start.10 = (f32[1,128,128]{1,2,0:T(8,128)S(1)}, f32[1,128,128]{1,2,0:T(8,128)S(1)}, u32[]{:S(2)}, u32[]{:S(2)}) collective-permute-start(f32[1,128,128]{1,2,0:T(8,128)S(1)} %bitcast.264), channel_id=1, source_target_pairs={{0,32},{4,36},{8,40},{12,44},{16,48},{20,52},{24,56},{28,60},{32,6... | collective-permute-start | bytes 196616 | tf_op jit(solution)/shard_map/ppermute | solution.py:84
  65.4 6.8 %collective-permute-start.11 = (f32[1,128,128]{1,2,0:T(8,128)S(1)}, f32[1,128,128]{1,2,0:T(8,128)S(1)}, u32[]{:S(2)}, u32[]{:S(2)}) collective-permute-start(f32[1,128,128]{1,2,0:T(8,128)S(1)} %fusion.31), channel_id=1, source_target_pairs={{0,64},{4,68},{8,72},{12,76},{16,80},{20,84},{24,88},{28,92},{32,9... | collective-permute-start | bytes 196616 | tf_op jit(solution)/shard_map/ppermute | solution.py:84
  72.5 14.0 %collective-permute-start.12 = (f32[1,128,128]{1,2,0:T(8,128)S(1)}, f32[1,128,128]{1,2,0:T(8,128)S(1)}, u32[]{:S(2)}, u32[]{:S(2)}) collective-permute-start(f32[1,128,128]{1,2,0:T(8,128)S(1)} %slice_select_fusion.1), channel_id=1, source_target_pairs={{0,128},{4,132},{8,136},{12,140},{16,144},{20,148},{24,152},{28,15... | collective-permute-start | bytes 196616 | tf_op jit(solution)/shard_map/ppermute | solution.py:84
  88.6 8.6 %collective-permute-start.13 = (f32[1,128,128]{2,1,0:T(8,128)S(1)}, f32[1,128,128]{2,1,0:T(8,128)S(1)}, u32[]{:S(2)}, u32[]{:S(2)}) collective-permute-start(f32[1,128,128]{2,1,0:T(8,128)S(1)} %get-tuple-element.13), channel_id=1, source_target_pairs={{0,4},{4,8},{8,12},{12,16},{16,20},{20,24},{24,28},{28,0},{32,36},... | collective-permute-start | bytes 196616 | tf_op jit(solution)/shard_map/ppermute | solution.py:108
  90.9 6.3 %collective-permute-start.14 = (f32[1,128,128]{2,1,0:T(8,128)S(1)}, f32[1,128,128]{2,1,0:T(8,128)S(1)}, u32[]{:S(2)}, u32[]{:S(2)}) collective-permute-start(f32[1,128,128]{2,1,0:T(8,128)S(1)} %get-tuple-element.12), channel_id=1, source_target_pairs={{0,8},{4,12},{8,16},{12,20},{16,24},{20,28},{24,0},{28,4},{32,40},... | collective-permute-start | bytes 196616 | tf_op jit(solution)/shard_map/ppermute | solution.py:108
  91.4 6.5 %collective-permute-start.15 = (f32[1,128,128]{2,1,0:T(8,128)S(1)}, f32[1,128,128]{2,1,0:T(8,128)S(1)}, u32[]{:S(2)}, u32[]{:S(2)}) collective-permute-start(f32[1,128,128]{2,1,0:T(8,128)S(1)} %get-tuple-element.11), channel_id=1, source_target_pairs={{0,12},{4,16},{8,20},{12,24},{16,28},{20,0},{24,4},{28,8},{32,44},... | collective-permute-start | bytes 196616 | tf_op jit(solution)/shard_map/ppermute | solution.py:108
  94.0 5.8 %collective-permute-start.16 = (f32[1,128,128]{2,1,0:T(8,128)S(1)}, f32[1,128,128]{2,1,0:T(8,128)S(1)}, u32[]{:S(2)}, u32[]{:S(2)}) collective-permute-start(f32[1,128,128]{2,1,0:T(8,128)S(1)} %get-tuple-element.10), channel_id=1, source_target_pairs={{0,16},{4,20},{8,24},{12,28},{16,0},{20,4},{24,8},{28,12},{32,48},... | collective-permute-start | bytes 196616 | tf_op jit(solution)/shard_map/ppermute | solution.py:108
  94.5 5.7 %collective-permute-start.17 = (f32[1,128,128]{2,1,0:T(8,128)S(1)}, f32[1,128,128]{2,1,0:T(8,128)S(1)}, u32[]{:S(2)}, u32[]{:S(2)}) collective-permute-start(f32[1,128,128]{2,1,0:T(8,128)S(1)} %get-tuple-element.9), channel_id=1, source_target_pairs={{0,20},{4,24},{8,28},{12,0},{16,4},{20,8},{24,12},{28,16},{32,52},... | collective-permute-start | bytes 196616 | tf_op jit(solution)/shard_map/ppermute | solution.py:108
  97.1 3.5 %collective-permute-start.18 = (f32[1,128,128]{2,1,0:T(8,128)S(1)}, f32[1,128,128]{2,1,0:T(8,128)S(1)}, u32[]{:S(2)}, u32[]{:S(2)}) collective-permute-start(f32[1,128,128]{2,1,0:T(8,128)S(1)} %get-tuple-element.8), channel_id=1, source_target_pairs={{0,24},{4,28},{8,0},{12,4},{16,8},{20,12},{24,16},{28,20},{32,56},... | collective-permute-start | bytes 196616 | tf_op jit(solution)/shard_map/ppermute | solution.py:108
  97.2 4.5 %collective-permute-start.19 = (f32[1,128,128]{2,1,0:T(8,128)S(1)}, f32[1,128,128]{2,1,0:T(8,128)S(1)}, u32[]{:S(2)}, u32[]{:S(2)}) collective-permute-start(f32[1,128,128]{2,1,0:T(8,128)S(1)} %get-tuple-element.7), channel_id=1, source_target_pairs={{0,28},{4,0},{8,4},{12,8},{16,12},{20,16},{24,20},{28,24},{32,60},... | collective-permute-start | bytes 196616 | tf_op jit(solution)/shard_map/ppermute | solution.py:108
  (1 other events, 2.4 us)
